TPU v7x, 32 devices: a whole 2x2x4 slice. The times are simulated.
32 devices in a mesh: req: 8 (over z, y), tp: 4 (over x, core).
Axes of the slice: x: 2, y: 2, z: 4, core: 2. Of those that a mesh axis runs over, the one named last changes fastest.
Arguments:
- hidden: bfloat16 [32, 128, 2304], P('req', None, 'tp')
- qkv: bfloat16 [32, 128, 4, 1024], P('req', None, 'tp')
- page_store: bfloat16 [16, 128, 4, 512], P('req', None, 'tp')
- page_owner: int32 [8], replicated, may hold values from 0 to 7, as said below
- page_slot: int32 [8], replicated, may hold values from 0 to 1
- lengths: int32 [32], replicated, may hold values from 1 to 128, 2048 in all
- request_perm: int32 [32], replicated, may hold values from 0 to 31, each once
- w_out: bfloat16 [2048, 2304], P(None, 'tp')
- post_gain: float32 [2304], P('tp'), may hold values from 0.25 to 1.75
Outputs:
- result: bfloat16 [32, 128, 2304], P('req', None, 'tp')
Inputs may be any that keep to these rules, and one draw needn't show every extreme that they name: Page p lies in slot page_slot[p] of the device with index page_owner[p] along req; no two pages share an owner.
All inputs are finite; a program needn't handle non-finite values.
Results may differ from a plain program's by a relative error of at most 0.0043.
Values may be sent and summed in bfloat16 or wider, within the bound.
No kernel may reach another device: no remote copies, remote signals or barrier semaphores. Data moves between devices by JAX's collectives and lax.ppermute only.
A program may use at most 64 MiB of HBM per device.

v0:
```python
import jax
import jax.numpy as jnp
from jax import lax
from jax.sharding import PartitionSpec as P

D = 2304
HD = 256
EPSILON = 1e-06
SOFT_CAP = 50.0


def tables(positions, width):
    half_width = width // 2
    frequency = 10000.0 ** (-(jnp.arange(half_width, dtype=jnp.float32) * 2.0 / width))
    angles = positions.astype(jnp.float32)[:, None] * frequency[None, :]
    return (jnp.cos(angles), jnp.sin(angles))


def rotate(values, cosine, sine):
    half_width = values.shape[-1] // 2
    first = values[..., :half_width]
    second = values[..., half_width:]
    return jnp.concatenate([first * cosine - second * sine, second * cosine + first * sine], -1)


def capped_exp(scores):
    return jnp.exp(SOFT_CAP * jnp.tanh(scores / SOFT_CAP))


def on_device(
    hidden, qkv, page_store, page_owner, page_slot, lengths, request_perm, w_out, post_gain
):
    requests, slots, local_width = hidden.shape
    groups = qkv.shape[2]
    per_group = qkv.shape[3] // HD - 2
    token_rows = requests * slots
    device_row = lax.axis_index("req")
    my_requests = lax.dynamic_slice_in_dim(request_perm, device_row * requests, requests)
    matches = my_requests[:, None] == jnp.arange(lengths.shape[0], dtype=jnp.int32)[None, :]
    my_lengths = jnp.sum(jnp.where(matches, lengths[None, :], 0), 1)
    position = jnp.arange(slots, dtype=jnp.int32)
    live_mask = (position[None, :] < my_lengths[:, None]).astype(jnp.float32)
    source = hidden.astype(jnp.float32)
    projections = qkv.astype(jnp.float32).reshape(requests, slots, groups, per_group + 2, HD)
    page_count = page_owner.shape[0]
    prefix_len = page_store.shape[1] * page_count
    cosine, sine = tables(prefix_len + position, HD)
    queries = (
        rotate(
            projections[:, :, :, :per_group],
            cosine[None, :, None, None, :],
            sine[None, :, None, None, :],
        )
        * HD ** (-0.5)
    ).astype(jnp.bfloat16)
    fresh_keys = rotate(
        projections[:, :, :, per_group], cosine[None, :, None, :], sine[None, :, None, :]
    ).astype(jnp.bfloat16)
    fresh_values = projections[:, :, :, per_group + 1].astype(jnp.bfloat16)
    picked = page_store[page_slot]
    held_here = page_owner == device_row
    offered = jnp.where(held_here[:, None, None, None], picked.astype(jnp.float32), 0.0)
    prefix = lax.psum(offered, "req").astype(jnp.bfloat16)
    prefix = prefix.reshape(prefix_len, groups, 2 * HD)
    prefix_keys = prefix[:, :, :HD]
    prefix_values = prefix[:, :, HD:]
    prefix_weights = capped_exp(
        jnp.einsum("rsgqh,tgh->rsgqt", queries, prefix_keys, preferred_element_type=jnp.float32)
    )
    allowed = (position[None, None, :] <= position[None, :, None]) & (
        position[None, None, :] < my_lengths[:, None, None]
    )
    suffix_raw = capped_exp(
        jnp.einsum("rsgqh,rtgh->rsgqt", queries, fresh_keys, preferred_element_type=jnp.float32)
    )
    suffix_weights = jnp.where(allowed[:, :, None, None, :], suffix_raw, 0.0)
    totals = jnp.sum(prefix_weights, -1) + jnp.sum(suffix_weights, -1)
    prefix_probs = (prefix_weights / totals[..., None]).astype(jnp.bfloat16)
    suffix_probs = (suffix_weights / totals[..., None]).astype(jnp.bfloat16)
    attended = jnp.einsum(
        "rsgqt,tgh->rsgqh", prefix_probs, prefix_values, preferred_element_type=jnp.float32
    )
    attended = attended + jnp.einsum(
        "rsgqt,rtgh->rsgqh", suffix_probs, fresh_values, preferred_element_type=jnp.float32
    )
    attended = attended.astype(jnp.bfloat16).reshape(token_rows, groups * per_group * HD)
    projected = jnp.dot(
        lax.all_gather(attended, "tp", axis=1, tiled=True),
        w_out,
        preferred_element_type=jnp.float32,
    )
    projected = projected.reshape(requests, slots, local_width)
    branch_total = lax.psum(jnp.sum(projected * projected, -1), "tp")
    branch = projected * lax.rsqrt(branch_total / D + EPSILON)[..., None] * post_gain
    return ((source + branch) * live_mask[..., None]).astype(jnp.bfloat16)


def solution(mesh):
    placed = (
        P("req", None, "tp"),
        P("req", None, "tp", None),
        P("req", None, "tp", None),
        P(),
        P(),
        P(),
        P(),
        P(None, "tp"),
        P("tp"),
    )
    return jax.shard_map(
        on_device, mesh=mesh, in_specs=placed, out_specs=P("req", None, "tp"), check_vma=False
    )
```

profile of v0, /device:TPU:0, one launch (start us, length us, event | category | flops | bytes accessed | tf_op | source)
XLA Modules:
  0.0 157.9 jit_solution(3614587715875364756)
XLA Ops:
  6.5 0.0 copy-start
  6.5 0.0 all-gather.2.cloned.1.call-start
  6.6 0.8 broadcast_compare_fusion
  7.4 0.7 compare_select_fusion
  8.1 0.7 dynamic_slice.3
  8.8 0.8 select_reduce_fusion
  9.6 0.1 fusion.36
  9.7 1.6 gather_fusion
  11.3 1.7 %convert_select_fusion = f32[8,128,1,512]{3,1,0,2:T(8,128)} fusion(bf16[8,128,512]{2,1,0:T(8,128)(2,1)S(1)} %gather_fusion, pred[8]{0:T(512)(128)(4,1)S(1)} %broadcast_compare_fusion), kind=kLoop, calls=%fused_computation.5 | loop fusion | flops 1048576 | bytes 3145736 | tf_op jit(solution)/shard_map/jit(_where)/select_n | solution.py:62
  13.0 0.0 copy-start.2
  13.0 95.0 %all-reduce.1 = bf16[8,128,1,512]{3,1,0,2:T(8,128)(2,1)} all-reduce(f32[8,128,1,512]{3,1,0,2:T(8,128)} %convert_select_fusion), channel_id=1, replica_groups=mesh['req'=8,'tp'=4] {'req'}, use_global_device_ids=true, to_apply=%region_0.1 | all-reduce | flops 524288 | bytes 3145728 | tf_op jit(solution)/shard_map/psum | solution.py:63
  108.0 0.0 copy-done.2
  108.0 1.3 copy.24
  109.3 1.5 copy.25
  110.8 0.2 reshape.303
  111.0 0.0 copy-start.1
  111.0 0.3 multiply_cosine_fusion
  111.4 0.1 subtract_bitcast_fusion
  111.5 0.1 fusion.25
  111.6 0.1 broadcast_and_fusion
  111.7 0.5 copy-done.1
  112.2 1.3 bitcast_reduce_fusion
  113.6 0.4 fusion.37
  114.0 1.5 fusion.6
  115.5 1.2 fusion.10
  116.7 0.5 copy.31
  117.2 0.9 copy.43
  118.1 0.0 all-gather.2.cloned.1.call-update
  118.1 0.0 copy-start.3
  118.1 21.8 %all-gather.2.cloned.1.call-done = bf16[512,2048]{1,0:T(8,128)(2,1)} async-done(((bf16[512,512]{1,0:T(8,128)(2,1)}), bf16[512,2048]{1,0:T(8,128)(2,1)}) %all-gather.2.cloned.1.call-update) | async-done | bytes 2097168 | tf_op jit(solution)/shard_map/all_gather | solution.py:88
  139.9 0.0 copy-done
  139.9 3.0 %multiply_reduce_fusion = (f32[512]{0:T(512)S(1)}, f32[512,576]{0,1:T(8,128)S(1)}) fusion(bf16[512,2048]{1,0:T(8,128)(2,1)} %all-gather.2.cloned.1.call-done, bf16[2048,576]{0,1:T(8,128)(2,1)S(1)} %copy-done), kind=kOutput, calls=%fused_computation.24 | convolution fusion | flops 1208548864 | bytes 5638144 | tf_op jit(solution)/shard_map/dot_general | solution.py:87
  143.0 5.9 %psum.15 = f32[4,128]{1,0:T(4,128)S(1)} all-reduce(f32[4,128]{1,0:T(4,128)S(1)} %bitcast.112), channel_id=1, replica_groups=mesh['req'=8,'tp'=4] {'tp'}, use_global_device_ids=true, to_apply=%region_5.6 | all-reduce | flops 512 | bytes 4096 | tf_op jit(solution)/shard_map/psum | solution.py:93
  148.9 0.0 copy-done.3
  148.9 2.2 %fusion.18 = bf16[4,128,576]{1,2,0:T(8,128)(2,1)} fusion(bf16[4,128,576]{1,2,0:T(8,128)(2,1)} %param.9, f32[4,128]{1,0:T(4,128)S(1)} %get-tuple-element.11, f32[576]{0:T(1024)S(1)} %copy-done.3, f32[4,128]{1,0:T(4,128)S(1)} %add_rsqrt_fusion, f32[512,576]{0,1:T(8,128)S(1)} %get-tuple-element.18), kind=kLoop, calls=%fused_computation.23 | loop fusion | flops 1769472 | bytes 2365696 | tf_op jit(solution)/shard_map/convert_element_type | solution.py:95
  (7 shorter events, 0.1 us)
Async XLA Ops:
  6.5 133.4 %copy-start = (bf16[2048,576]{0,1:T(8,128)(2,1)S(1)}, bf16[2048,576]{0,1:T(8,128)(2,1)}, u32[]{:S(2)}) copy-start(bf16[2048,576]{0,1:T(8,128)(2,1)} %param.16) | copy-start | bytes 7077892
  6.5 133.4 %all-gather.2.cloned.1.call-start = ((), (), s32[]{:S(2)}) async-start(), calls=%async_computation | async-start | bytes 2621440 | tf_op jit(solution)/shard_map/all_gather | solution.py:88
  13.0 95.0 %copy-start.2 = (bf16[4,128,1,1024]{3,1,2,0:T(8,128)(2,1)S(1)}, bf16[4,128,1,1024]{3,1,2,0:T(8,128)(2,1)}, u32[]{:S(2)}) copy-start(bf16[4,128,1,1024]{3,1,2,0:T(8,128)(2,1)} %param.10) | copy-start | bytes 3145732
  111.0 1.2 copy-start.1
  118.1 30.8 %copy-start.3 = (f32[576]{0:T(1024)S(1)}, f32[576]{0:T(1024)}, u32[]{:S(2)}) copy-start(f32[576]{0:T(1024)} %param.17) | copy-start | bytes 6916
Sparse Core Ops, SparseCore 0:
  118.2 21.6 all-gather.1
where the time goes:
time: 158 us
  blocking collectives  101 us (64%)
  waiting for transfers between devices  21.9 us (14%)
  between operations  13.5 us (9%)
  matrix products  7.48 us (5%)
  other arithmetic  7.23 us (5%)
  local copies, waits for them, and re-layouts  6.97 us (4%)
    psum x1, blocking collectives, on_device(): prefix = lax.psum(offered, 'req').astype(jnp.bfloat16)  95 us
    all_gather x1, waiting for transfers between devices, on_device(): lax.all_gather(attended, 'tp', axis=1, tiled=True)  21.8 us
    psum x1, blocking collectives, on_device(): branch_total = lax.psum(jnp.sum(projected * projected, -1), 'tp')  5.89 us
  transfers between devices with their start and end apart: 1, of which 1 were waited for; matrix products, arithmetic and copies ran while one was open for 0% of the time, Pallas kernels for 0%

commit v1 on v0

--- a/solution.py
+++ b/solution.py
@@ -1,3 +1,4 @@
+import functools
 import jax
 import jax.numpy as jnp
 from jax import lax
@@ -7,6 +8,27 @@
 HD = 256
 EPSILON = 1e-06
 SOFT_CAP = 50.0
+
+
+def balance_face(own_rows, which_axis, in_dim):
+    workers = lax.axis_size(which_axis)
+    mixed_arr = range(workers)
+    w1 = map(lambda p: (p, (p + 1) % workers), mixed_arr)
+    ledger = list(map(lambda p: (p, (p - 1) % workers), range(workers)))
+    mat_out, answer = ([own_rows], [own_rows])
+    column = list(w1)
+    for _ in range(workers // 2):
+        ready = lax.ppermute(mat_out[-1], axis_name=which_axis, perm=column)
+        mat_out.append(ready)
+    for _ in tuple(range((workers - 1) // 2)):
+        answer.append(lax.ppermute(answer[-1], axis_name=which_axis, perm=ledger))
+    inter = jnp.concatenate([*mat_out[::-1], *answer[1:]], axis=in_dim)
+    right_arr = lax.axis_index(which_axis)
+    upper = jnp.roll(inter, shift=(right_arr - workers // 2) * own_rows.shape[in_dim], axis=in_dim)
+    return upper
+
+
+_part_modes = functools.partial(balance_face, which_axis="tp", in_dim=1)
 
 
 def tables(positions, width):
@@ -84,11 +106,7 @@
         "rsgqt,rtgh->rsgqh", suffix_probs, fresh_values, preferred_element_type=jnp.float32
     )
     attended = attended.astype(jnp.bfloat16).reshape(token_rows, groups * per_group * HD)
-    projected = jnp.dot(
-        lax.all_gather(attended, "tp", axis=1, tiled=True),
-        w_out,
-        preferred_element_type=jnp.float32,
-    )
+    projected = jnp.dot(_part_modes(attended), w_out, preferred_element_type=jnp.float32)
     projected = projected.reshape(requests, slots, local_width)
     branch_total = lax.psum(jnp.sum(projected * projected, -1), "tp")
     branch = projected * lax.rsqrt(branch_total / D + EPSILON)[..., None] * post_gain

time: 158 us -> 149 us (0.943)
  between operations: 13.5 us -> 0.23 us
  local copies, waits for them, and re-layouts: 6.97 us -> 11.5 us
  waiting for transfers between devices: 21.9 us -> 19.4 us
  starting transfers between devices: 0.01 us -> 1.8 us
    all_gather x1 -> x0, waiting for transfers between devices: 21.8 us -> none  [on_device(): lax.all_gather(attended, 'tp', axis=1, tiled=True)]
    ppermute x0 -> x3, waiting for transfers between devices: none -> 19.4 us  [the longest x2 19.4 us: balance_face(): ready = lax.ppermute(mat_out[-1], axis_name=which_axis, perm=column)]
    unnamed x10 -> x15, local copies, waits for them, and re-layouts: 2.71 us -> 6.16 us
    ppermute x0 -> x3, starting transfers between devices: none -> 1.8 us  [the longest x1 1.74 us: balance_face(): answer.append(lax.ppermute(answer[-1], axis_name=which_axis, perm=ledger))]
  transfers between devices with their start and end apart: 1 -> 3, of which waited for: 1 -> 2; matrix products, arithmetic and copies ran while one was open for 0% -> 1% of each run, Pallas kernels for 0% -> 0%
where the time goes in v1:
time: 149 us; the launch traced here: 148 us
  blocking collectives  102 us (68%)
  waiting for transfers between devices  19.4 us (13%)
  local copies, waits for them, and re-layouts  11.5 us (8%)
  other arithmetic  7.18 us (5%)
  matrix products  5.97 us (4%)
  starting transfers between devices  1.8 us (1%)
    psum x1, blocking collectives, on_device(): prefix = lax.psum(offered, 'req').astype(jnp.bfloat16)  94.8 us
    ppermute x2, waiting for transfers between devices, balance_face(): ready = lax.ppermute(mat_out[-1], axis_name=which_axis, perm=column)  19.4 us
    psum x1, blocking collectives, on_device(): branch_total = lax.psum(jnp.sum(projected * projected, -1), 'tp')  7.04 us
    unnamed x15, local copies, waits for them, and re-layouts  6.16 us
  transfers between devices with their start and end apart: 3, of which 2 were waited for; matrix products, arithmetic and copies ran while one was open for 1% of the time, Pallas kernels for 0%

profile of v1, /device:TPU:0, one launch (start us, length us, event | category | flops | bytes accessed | tf_op | source)
XLA Modules:
  0.0 148.0 jit_solution(11768755042611466080)
XLA Ops:
  0.0 0.0 copy-start
  0.0 0.8 broadcast_compare_fusion
  0.9 0.7 compare_select_fusion
  1.5 0.7 dynamic_slice.7
  2.2 0.8 select_reduce_fusion
  3.1 0.1 fusion.39
  3.2 1.6 %gather_fusion = bf16[8,128,512]{2,1,0:T(8,128)(2,1)S(1)} fusion(bf16[2,128,512]{2,1,0:T(8,128)(2,1)} %bitcast.108, s32[1024]{0:T(1024)S(1)} %pad_clamp_fusion), kind=kCustom, calls=%fused_computation | custom fusion | bytes 2097184 | tf_op jit(solution)/shard_map/gather | solution.py:82
  4.7 1.7 %convert_select_fusion = f32[8,128,1,512]{3,1,0,2:T(8,128)} fusion(bf16[8,128,512]{2,1,0:T(8,128)(2,1)S(1)} %gather_fusion, pred[8]{0:T(512)(128)(4,1)S(1)} %broadcast_compare_fusion), kind=kLoop, calls=%fused_computation.5 | loop fusion | flops 1048576 | bytes 3145736 | tf_op jit(solution)/shard_map/jit(_where)/select_n | solution.py:84
  6.5 94.8 %all-reduce.1 = bf16[8,128,1,512]{3,1,0,2:T(8,128)(2,1)} all-reduce(f32[8,128,1,512]{3,1,0,2:T(8,128)} %convert_select_fusion), channel_id=1, replica_groups=mesh['req'=8,'tp'=4] {'req'}, use_global_device_ids=true, to_apply=%region_0.1 | all-reduce | flops 524288 | bytes 3145728 | tf_op jit(solution)/shard_map/psum | solution.py:85
  101.3 2.3 %copy.24 = bf16[4,128,1,1024]{1,3,0,2:T(8,128)(2,1)} copy(bf16[4,128,1,1024]{3,1,2,0:T(8,128)(2,1)} %param.10) | data formatting | bytes 2097152 | tf_op args[1]
  103.6 1.5 %copy.25 = bf16[4,128,1,4,256]{4,1,3,0,2:T(8,128)(2,1)S(1)} copy(bf16[4,128,1,4,256]{1,4,3,0,2:T(8,128)(2,1)} %bitcast.109) | data formatting | bytes 2097152 | tf_op jit(solution)/shard_map/reshape | solution.py:66
  105.1 0.0 copy-start.1
  105.1 0.2 reshape.303
  105.3 0.3 multiply_cosine_fusion
  105.7 0.1 subtract_bitcast_fusion
  105.8 0.1 fusion.27
  105.9 0.1 broadcast_and_fusion
  106.0 0.3 copy-done.1
  106.3 1.3 bitcast_reduce_fusion
  107.6 0.4 fusion.40
  108.0 1.5 %fusion.8 = f32[4,128,1,2,256]{1,4,3,0,2:T(8,128)S(1)} fusion(f32[4,128,2]{1,2,0:T(2,128)S(1)} %add.78, f32[1024,4,128,2]{2,0,3,1:T(8,128)S(1)} %get-tuple-element.14, bf16[1024,1,512]{2,0,1:T(8,128)(2,1)S(1)} %bitcast.113), kind=kOutput, calls=%fused_computation.13 | convolution fusion | flops 541065216 | bytes 5771264 | tf_op jit(solution)/shard_map/rsgqt,tgh->rsgqh/dot_general | solution.py:102
  109.5 1.3 fusion.12
  110.8 0.5 copy.31
  111.2 0.1 copy.43
  111.3 0.1 collective-permute-start
  111.4 8.6 %collective-permute-done = bf16[512,512]{1,0:T(8,128)(2,1)S(1)} collective-permute-done((bf16[512,512]{1,0:T(8,128)(2,1)S(1)}, bf16[512,512]{1,0:T(8,128)(2,1)S(1)}, u32[]{:S(2)}, u32[]{:S(2)}) %collective-permute-start) | collective-permute-done | bytes 524320 | tf_op jit(solution)/shard_map/ppermute | solution.py:21
  120.0 0.0 collective-permute-start.1
  120.0 1.7 %collective-permute-start.2 = (bf16[512,512]{1,0:T(8,128)(2,1)S(1)}, bf16[512,512]{1,0:T(8,128)(2,1)}, u32[]{:S(2)}, u32[]{:S(2)}) collective-permute-start(bf16[512,512]{1,0:T(8,128)(2,1)S(1)} %bitcast.105), channel_id=1, source_target_pairs={{0,3},{1,0},{2,1},{3,2},{4,7},{5,4},{6,5},{7,6},{8,11},{9,8},{10,9... | collective-permute-start | bytes 1572872 | tf_op jit(solution)/shard_map/ppermute | solution.py:24
  121.7 10.8 %collective-permute-done.1 = bf16[512,512]{1,0:T(8,128)(2,1)} collective-permute-done((bf16[512,512]{1,0:T(8,128)(2,1)S(1)}, bf16[512,512]{1,0:T(8,128)(2,1)}, u32[]{:S(2)}, u32[]{:S(2)}) %collective-permute-start.1) | collective-permute-done | bytes 524320 | tf_op jit(solution)/shard_map/ppermute | solution.py:21
  132.5 1.1 constant_dynamic-update-slice_fusion.7
  133.6 0.1 constant_dynamic-update-slice_fusion.6
  133.7 0.1 constant_dynamic-update-slice_fusion.5
  133.8 0.0 collective-permute-done.2
  133.8 1.1 constant_dynamic-update-slice_fusion.4
  134.9 1.1 constant_dynamic-update-slice_fusion.3
  136.0 0.1 constant_dynamic-update-slice_fusion.2
  136.0 0.1 constant_dynamic-update-slice_fusion.1
  136.1 1.1 constant_dynamic-update-slice_fusion
  137.2 0.0 copy-done
  137.2 0.0 copy-start.2
  137.2 1.5 %multiply_reduce_fusion = (f32[512]{0:T(512)S(1)}, f32[512,576]{0,1:T(8,128)S(1)}) fusion(bf16[2048,576]{0,1:T(8,128)(2,1)S(1)} %copy-done, bf16[512,4096]{1,0:T(8,128)(2,1)S(1)} %constant_dynamic-update-slice_fusion, s32[]{:T(128)S(6)} %select_n.45), kind=kOutput, calls=%fused_computation.26 | convolution fusion | flops 1208548864 | bytes 5638148 | tf_op jit(solution)/shard_map/dot_general | solution.py:109
  138.8 7.0 %psum.15 = f32[4,128]{1,0:T(4,128)S(1)} all-reduce(f32[4,128]{1,0:T(4,128)S(1)} %bitcast.114), channel_id=1, replica_groups=mesh['req'=8,'tp'=4] {'tp'}, use_global_device_ids=true, to_apply=%region_5.6 | all-reduce | flops 512 | bytes 4096 | tf_op jit(solution)/shard_map/psum | solution.py:111
  145.8 0.0 copy-done.2
  145.8 2.2 %fusion.20 = bf16[4,128,576]{1,2,0:T(8,128)(2,1)} fusion(bf16[4,128,576]{1,2,0:T(8,128)(2,1)} %param.9, f32[4,128]{1,0:T(4,128)S(1)} %get-tuple-element.11, f32[576]{0:T(1024)S(1)} %copy-done.2, f32[4,128]{1,0:T(4,128)S(1)} %add_rsqrt_fusion, f32[512,576]{0,1:T(8,128)S(1)} %get-tuple-element.18), kind=kLoop, calls=%fused_computation.25 | loop fusion | flops 1769472 | bytes 2365696 | tf_op jit(solution)/shard_map/convert_element_type | solution.py:113
  (7 shorter events, 0.1 us)
Async XLA Ops:
  0.0 137.2 %copy-start = (bf16[2048,576]{0,1:T(8,128)(2,1)S(1)}, bf16[2048,576]{0,1:T(8,128)(2,1)}, u32[]{:S(2)}) copy-start(bf16[2048,576]{0,1:T(8,128)(2,1)} %param.16) | copy-start | bytes 7077892
  105.1 1.2 copy-start.1
  111.3 8.7 %collective-permute-start = (bf16[512,512]{1,0:T(8,128)(2,1)S(1)}, bf16[512,512]{1,0:T(8,128)(2,1)S(1)}, u32[]{:S(2)}, u32[]{:S(2)}) collective-permute-start(bf16[512,512]{1,0:T(8,128)(2,1)S(1)} %bitcast.104), channel_id=1, source_target_pairs={{0,1},{1,2},{2,3},{3,0},{4,5},{5,6},{6,7},{7,4},{8,9},{9,10},{10,1... | collective-permute-start | bytes 1572872 | tf_op jit(solution)/shard_map/ppermute | solution.py:21
  120.0 12.5 %collective-permute-start.1 = (bf16[512,512]{1,0:T(8,128)(2,1)S(1)}, bf16[512,512]{1,0:T(8,128)(2,1)}, u32[]{:S(2)}, u32[]{:S(2)}) collective-permute-start(bf16[512,512]{1,0:T(8,128)(2,1)S(1)} %collective-permute-done), channel_id=1, source_target_pairs={{0,1},{1,2},{2,3},{3,0},{4,5},{5,6},{6,7},{7,4},{8,9},{9,10},{10,1... | collective-permute-start | bytes 1572872 | tf_op jit(solution)/shard_map/ppermute | solution.py:21
  120.0 13.8 %collective-permute-start.2 = (bf16[512,512]{1,0:T(8,128)(2,1)S(1)}, bf16[512,512]{1,0:T(8,128)(2,1)}, u32[]{:S(2)}, u32[]{:S(2)}) collective-permute-start(bf16[512,512]{1,0:T(8,128)(2,1)S(1)} %bitcast.105), channel_id=1, source_target_pairs={{0,3},{1,0},{2,1},{3,2},{4,7},{5,4},{6,5},{7,6},{8,11},{9,8},{10,9... | collective-permute-start | bytes 1572872 | tf_op jit(solution)/shard_map/ppermute | solution.py:24
  137.2 8.6 %copy-start.2 = (f32[576]{0:T(1024)S(1)}, f32[576]{0:T(1024)}, u32[]{:S(2)}) copy-start(f32[576]{0:T(1024)} %param.17) | copy-start | bytes 6916
